TPU v7x, 32 devices: a whole 2x2x4 slice. The times are simulated.
32 devices in a mesh: groups: 2 (over x), tok: 16 (over z, y, core).
Axes of the slice: x: 2, y: 2, z: 4, core: 2. Of those that a mesh axis runs over, the one named last changes fastest.
Arguments:
- queries: bfloat16 [2, 8192, 1024], P(None, ('groups', 'tok')), parts along dimension 1, may hold values from -6 to 6
- keys: bfloat16 [2, 8192, 1024], P(None, ('groups', 'tok')), parts along dimension 1, may hold values from -6 to 6
- values: bfloat16 [2, 8192, 1024], P(None, ('groups', 'tok')), parts along dimension 1, may hold values from -6 to 6
- rates: float32 [2, 3, 2, 8192], P(None, None, None, ('groups', 'tok')), parts along dimension 3, may hold values from 0.0002 to 0.002
- fast_weights: float32 [2, 3, 512, 512], P(None, None, 'tok'), may hold values from -0.25 to 0.25
Outputs:
- attended: bfloat16 [2, 8192, 1024], P(None, ('groups', 'tok')), parts along dimension 1
- final_weights: float32 [4, 3, 512, 512], P('groups', None, 'tok'), parts along dimension 0
There are 2 independent parts, one for each index of `groups`. A program takes and returns all parts, laid end to end along the dimension named above; an argument that names none is the same for every part. Nothing has to cross between parts.
All inputs are finite; a program needn't handle non-finite values.
Results may differ from a plain program's by a relative error of at most 0.0098.
Values may be sent and summed in bfloat16 or wider, within the bound.
No kernel may reach another device: no remote copies, remote signals or barrier semaphores. Data moves between devices by JAX's collectives and lax.ppermute only.
A program may use at most 64 MiB of HBM per device.

v0:
```python
import jax
import jax.numpy as jnp
from jax import lax
from jax.sharding import PartitionSpec as P


def cross(left, right):
    return lax.dot_general(
        left, right, (((1,), (1,)), ((), ())), preferred_element_type=jnp.float32
    )


def inner(left, right):
    return lax.dot_general(
        left, right, (((0,), (0,)), ((), ())), preferred_element_type=jnp.float32
    )


def renorm(old, upd):
    old_norm = jnp.sqrt(jnp.mean(old * old, axis=-1))
    new_norm = jnp.sqrt(jnp.mean(upd * upd, axis=-1) + 1e-06)
    return upd * (old_norm / new_norm)[..., None]


def head_step(query, key_rows, value_rows, rate_rows, wbf):
    hidden_q = (jax.nn.silu(cross(query, wbf[0])) * cross(query, wbf[1])).astype(jnp.bfloat16)
    raw = cross(hidden_q, wbf[2])
    normed = (raw / jnp.sqrt(jnp.mean(raw * raw, axis=-1, keepdims=True) + 1e-06)).astype(
        jnp.bfloat16
    )
    h1 = cross(key_rows, wbf[0])
    h3 = cross(key_rows, wbf[1])
    sig = jax.nn.sigmoid(h1)
    act = h1 * sig
    back = jnp.dot(value_rows, wbf[2], preferred_element_type=jnp.float32)
    d1 = back * h3 * sig * (1.0 + h1 * (1.0 - sig))
    d3 = back * act
    e1 = (rate_rows[0][:, None] * d1).astype(jnp.bfloat16)
    e3 = (rate_rows[1][:, None] * d3).astype(jnp.bfloat16)
    b2 = (rate_rows[2][:, None] * (act * h3)).astype(jnp.bfloat16)
    grad = jnp.stack([inner(e1, key_rows), inner(e3, key_rows), inner(value_rows, b2)])
    return (normed, grad)


def block_step(span, gathered, queries, keys, values, rates):
    heads = gathered.shape[0]
    width = gathered.shape[3]
    pieces = []
    grads = []
    for head in range(heads):
        lo = head * width
        normed, grad = head_step(
            queries[span][:, lo : lo + width],
            keys[span][:, lo : lo + width],
            values[span][:, lo : lo + width],
            rates[span][:, head],
            gathered[head],
        )
        pieces.append(normed)
        grads.append(grad)
    return (jnp.concatenate(pieces, axis=1), jnp.stack(grads))


def fetch(own):
    return lax.all_gather(own.astype(jnp.bfloat16), "tok", axis=2, tiled=True)


def settle(partial_value, own):
    total = lax.psum_scatter(partial_value, "tok", scatter_dimension=2, tiled=True)
    return renorm(own, own + total)


def on_device(queries, keys, values, rates, fast_weights):
    nblocks = queries.shape[0]
    own = fast_weights
    blocks = []
    for span in range(nblocks):
        gathered = fetch(own)
        normed, partial_value = block_step(span, gathered, queries, keys, values, rates)
        blocks.append(normed)
        own = settle(partial_value, own)
    return (jnp.stack(blocks), own)


def solution(mesh):
    placed = (
        P(None, ("groups", "tok"), None),
        P(None, ("groups", "tok"), None),
        P(None, ("groups", "tok"), None),
        P(None, None, None, ("groups", "tok")),
        P(None, None, "tok", None),
    )
    return jax.shard_map(
        on_device,
        mesh=mesh,
        in_specs=placed,
        out_specs=(P(None, ("groups", "tok"), None), P("groups", None, "tok", None)),
        check_vma=False,
    )
```

profile of v0, /device:TPU:0, one launch (start us, length us, event | category | flops | bytes accessed | tf_op | source)
XLA Modules:
  0.0 308.0 jit_solution(13420339890189697955)
XLA Ops:
  7.2 1.9 multiply_reduce_fusion.7
  10.5 2.2 slice_bitcast_fusion.12
  12.8 1.1 slice_bitcast_fusion.13
  13.8 45.2 %all-gather.3.cloned.1.call-done = bf16[2,3,512,512]{3,2,1,0:T(8,128)(2,1)} async-done(((bf16[2,3,32,512]{3,2,1,0:T(8,128)(2,1)}), bf16[2,3,512,512]{3,2,1,0:T(8,128)(2,1)}) %all-gather.3.cloned.1.call-update) | async-done | bytes 3145744 | tf_op jit(solution)/shard_map/all_gather | solution.py:65
  59.0 1.6 fusion.34
  60.6 1.4 fusion.37
  62.0 1.4 convolution_bitcast_fusion.10
  68.0 3.4 %pad_maximum_fusion = f32[2,3,512,512]{3,2,1,0:T(8,128)} fusion(f32[1,3,512,512]{3,2,1,0:T(8,128)S(1)} %maximum_bitcast_fusion.1, f32[1,3,512,512]{3,2,1,0:T(8,128)S(1)} %maximum_bitcast_fusion), kind=kLoop, calls=%fused_computation | loop fusion | flops 1572864 | bytes 12582912 | tf_op jit(solution)/shard_map/stack | solution.py:61
  71.5 83.5 %reduce-scatter.3.cloned.1.call-done = f32[2,3,32,512]{3,2,1,0:T(8,128)} async-done(((f32[2,3,512,512]{3,2,1,0:T(8,128)}), f32[2,3,32,512]{3,2,1,0:T(8,128)}) %reduce-scatter.3.cloned.1.call-update) | async-done | bytes 393232 | tf_op jit(solution)/shard_map/reduce_scatter | solution.py:69
  155.0 1.2 multiply_reduce_fusion.6
  157.2 45.1 %all-gather.5.cloned.1.call-done = bf16[2,3,512,512]{3,2,1,0:T(8,128)(2,1)} async-done(((bf16[2,3,32,512]{3,2,1,0:T(8,128)(2,1)}), bf16[2,3,512,512]{3,2,1,0:T(8,128)(2,1)}) %all-gather.5.cloned.1.call-update) | async-done | bytes 3145744 | tf_op jit(solution)/shard_map/all_gather | solution.py:65
  202.4 1.6 convolution_bitcast_fusion.16
  204.0 1.4 convolution_bitcast_fusion.13
  205.4 1.4 convolution_bitcast_fusion.4
  211.4 3.4 %pad_maximum_fusion.1 = f32[2,3,512,512]{3,2,1,0:T(8,128)} fusion(f32[1,3,512,512]{3,2,1,0:T(8,128)S(1)} %maximum_bitcast_fusion.3, f32[1,3,512,512]{3,2,1,0:T(8,128)S(1)} %maximum_bitcast_fusion.2), kind=kLoop, calls=%fused_computation.1 | loop fusion | flops 1572864 | bytes 12582912 | tf_op jit(solution)/shard_map/stack | solution.py:61
  214.8 2.1 slice_bitcast_fusion.17
  217.6 1.2 fusion.39
  218.8 2.5 multiply_reduce_fusion.2
  221.3 2.1 fusion.35
  223.4 2.5 multiply_reduce_fusion.3
  226.0 1.6 divide_convert_fusion.2
  227.5 0.9 maximum_bitcast_fusion.4
  228.4 2.3 convolution_bitcast_fusion.19
  230.7 2.5 multiply_reduce_fusion
  233.2 2.1 convolution_bitcast_fusion.21
  235.3 2.5 multiply_reduce_fusion.1
  237.8 1.1 divide_convert_fusion
  239.0 1.1 divide_convert_fusion.1
  240.2 2.1 pad_maximum_fusion.2
  242.3 56.0 %reduce-scatter.5.cloned.1.call-done = f32[2,3,32,512]{3,2,1,0:T(8,128)} async-done(((f32[2,3,512,512]{3,2,1,0:T(8,128)}), f32[2,3,32,512]{3,2,1,0:T(8,128)}) %reduce-scatter.5.cloned.1.call-update) | async-done | bytes 393232 | tf_op jit(solution)/shard_map/reduce_scatter | solution.py:69
  298.3 1.2 multiply_reduce_fusion.5
  299.6 1.9 broadcast_multiply_fusion
  (64 shorter events, 12.3 us)
Async XLA Ops:
  7.2 5.6 %copy-start.8 = (bf16[2,256,1024]{2,1,0:T(8,128)(2,1)S(1)}, bf16[2,256,1024]{2,1,0:T(8,128)(2,1)}, u32[]{:S(2)}) copy-start(bf16[2,256,1024]{2,1,0:T(8,128)(2,1)} %param.7) | copy-start | bytes 3145732
  7.2 51.8 %all-gather.3.cloned.1.call-start = ((), (), s32[]{:S(2)}) async-start(), calls=%async_computation.2 | async-start | bytes 3342336 | tf_op jit(solution)/shard_map/all_gather | solution.py:65
  9.2 145.8 %reduce-scatter.3.cloned.1.call-start = ((), (), s32[]{:S(2)}) async-start(), calls=%async_computation.3 | async-start | bytes 6684672 | tf_op jit(solution)/shard_map/reduce_scatter | solution.py:69
  59.0 4.5 %copy-start = (bf16[2,3,512,512]{3,2,1,0:T(8,128)(2,1)S(1)}, bf16[2,3,512,512]{3,2,1,0:T(8,128)(2,1)}, u32[]{:S(2)}) copy-start(bf16[2,3,512,512]{3,2,1,0:T(8,128)(2,1)} %all-gather.3.cloned.1.call-done) | copy-start | bytes 9437188
  59.0 4.5 %copy-start.4 = (bf16[256,1024]{1,0:T(8,128)(2,1)S(1)}, bf16[256,1024]{1,0:T(8,128)(2,1)}, u32[]{:S(2)}) copy-start(bf16[256,1024]{1,0:T(8,128)(2,1)} %get-tuple-element.9) | copy-start | bytes 1572868
  63.5 1.0 copy-start.6
  71.4 131.0 %all-gather.5.cloned.1.call-start = ((), (), s32[]{:S(2)}) async-start(), calls=%async_computation.4 | async-start | bytes 3342336 | tf_op jit(solution)/shard_map/all_gather | solution.py:65
  157.0 141.3 %reduce-scatter.5.cloned.1.call-start = ((), (), s32[]{:S(2)}) async-start(), calls=%async_computation.5 | async-start | bytes 6684672 | tf_op jit(solution)/shard_map/reduce_scatter | solution.py:69
  202.4 4.5 %copy-start.1 = (bf16[2,3,512,512]{3,2,1,0:T(8,128)(2,1)S(1)}, bf16[2,3,512,512]{3,2,1,0:T(8,128)(2,1)}, u32[]{:S(2)}) copy-start(bf16[2,3,512,512]{3,2,1,0:T(8,128)(2,1)} %all-gather.5.cloned.1.call-done) | copy-start | bytes 9437188
  202.4 4.5 %copy-start.3 = (bf16[256,1024]{1,0:T(8,128)(2,1)S(1)}, bf16[256,1024]{1,0:T(8,128)(2,1)}, u32[]{:S(2)}) copy-start(bf16[256,1024]{1,0:T(8,128)(2,1)} %get-tuple-element.8) | copy-start | bytes 1572868
  204.0 3.2 %copy-start.11 = (f32[1,1,256]{2,1,0:T(1,128)S(1)}, f32[1,1,256]{2,1,0:T(1,128)}, u32[]{:S(2)}) copy-start(f32[1,1,256]{2,1,0:T(1,128)} %get-tuple-element.16) | copy-start | bytes 3076
  206.8 1.0 copy-start.5
  206.9 1.0 copy-start.10
  207.7 1.3 copy-start.9
  216.9 0.8 copy-start.7
  225.9 4.8 %copy-start.2 = (bf16[2,3,512,512]{3,2,1,0:T(8,128)(2,1)S(1)}, bf16[2,3,512,512]{3,2,1,0:T(8,128)(2,1)}, u32[]{:S(2)}) copy-start(bf16[2,3,512,512]{3,2,1,0:T(8,128)(2,1)} %all-gather.5.cloned.1.call-done) | copy-start | bytes 9437188
Sparse Core Ops, SparseCore 0:
  10.7 48.2 all-gather.2
  71.5 83.3 reduce-scatter.2
  157.7 44.6 all-gather.4
  214.9 83.3 reduce-scatter.4
where the time goes:
time: 309 us; the launch traced here: 308 us
  waiting for transfers between devices  230 us (74%)
  matrix products  33.9 us (11%)
  other arithmetic  22 us (7%)
  between operations  14.1 us (5%)
  local copies, waits for them, and re-layouts  7.79 us (3%)
    reduce_scatter x2, waiting for transfers between devices, settle(): lax.psum_scatter(partial_value, 'tok', scatter_dimension=2, tiled=True)  140 us
    all_gather x2, waiting for transfers between devices, fetch(): return lax.all_gather(own.astype(jnp.bfloat16), 'tok', axis=2, tiled=True)  90.3 us
    dot_general x16, matrix products, cross(): lax.dot_general(left, right, (((1,), (1,)), ((), ())), preferred_element_...  22.8 us
    another operation x6, other arithmetic, block_step(): return (jnp.concatenate(pieces, axis=1), jnp.stack(grads))  7.97 us
    dot_general x12, matrix products, inner(): lax.dot_general(left, right, (((0,), (0,)), ((), ())), preferred_element_...  7.62 us
  transfers between devices with their start and end apart: 4, of which 4 were waited for; matrix products, arithmetic and copies ran while one was open for 10% of the time, Pallas kernels for 0%

commit v1 on v0

--- a/solution.py
+++ b/solution.py
@@ -2,6 +2,24 @@
 import jax.numpy as jnp
 from jax import lax
 from jax.sharding import PartitionSpec as P
+
+
+def ring_gather(array, axis, dim):
+    ways, here, turn = (lax.axis_size(axis), lax.axis_index(axis), array.shape[dim])
+    shape = [n * ways if d == dim else n for d, n in enumerate(array.shape)]
+    full = lax.dynamic_update_slice_in_dim(
+        jnp.zeros(shape, array.dtype), array, here * turn, axis=dim
+    )
+    going_up = going_down = array
+    for far in range(1, ways // 2 + 1):
+        going_up = lax.ppermute(going_up, axis, [(d, (d + 1) % ways) for d in range(ways)])
+        full = lax.dynamic_update_slice_in_dim(full, going_up, (here - far) % ways * turn, axis=dim)
+        if 2 * far < ways:
+            going_down = lax.ppermute(going_down, axis, [(d, (d - 1) % ways) for d in range(ways)])
+            full = lax.dynamic_update_slice_in_dim(
+                full, going_down, (here + far) % ways * turn, axis=dim
+            )
+    return full
 
 
 def cross(left, right):
@@ -62,7 +80,7 @@
 
 
 def fetch(own):
-    return lax.all_gather(own.astype(jnp.bfloat16), "tok", axis=2, tiled=True)
+    return ring_gather(own.astype(jnp.bfloat16), "tok", 2)
 
 
 def settle(partial_value, own):

time: 309 us -> 333 us (1.078)
  starting transfers between devices: 0.34 us -> 63.8 us
  waiting for transfers between devices: 230 us -> 194 us
  matrix products: 33.9 us -> 29.5 us
    all_gather x2 -> x0, waiting for transfers between devices: 90.3 us -> none  [fetch(): return lax.all_gather(own.astype(jnp.bfloat16), 'tok', axis=2, tiled=True)]
    ppermute x0 -> x30, starting transfers between devices: none -> 63.7 us  [the longest x14 63.1 us: ring_gather(): lax.ppermute(going_down, axis, [(d, (d - 1) % ways) for d in range(ways)])]
    ppermute x0 -> x30, waiting for transfers between devices: none -> 58.9 us  [the longest x16 58.9 us: ring_gather(): lax.ppermute(going_up, axis, [(d, (d + 1) % ways) for d in range(ways)])]
    reduce_scatter x2, waiting for transfers between devices: 140 us -> 136 us  [settle(): lax.psum_scatter(partial_value, 'tok', scatter_dimension=2, tiled=True)]
  transfers between devices with their start and end apart: 4 -> 32, of which waited for: 4 -> 17; matrix products, arithmetic and copies ran while one was open for 10% -> 11% of each run, Pallas kernels for 0% -> 0%
where the time goes in v1:
time: 333 us; the launch traced here: 332 us
  waiting for transfers between devices  194 us (58%)
  starting transfers between devices  63.8 us (19%)
  matrix products  29.5 us (9%)
  other arithmetic  19.9 us (6%)
  between operations  14.7 us (4%)
  local copies, waits for them, and re-layouts  9.81 us (3%)
    reduce_scatter x2, waiting for transfers between devices, settle(): lax.psum_scatter(partial_value, 'tok', scatter_dimension=2, tiled=True)  136 us
    ppermute x14, starting transfers between devices, ring_gather(): lax.ppermute(going_down, axis, [(d, (d - 1) % ways) for d in range(ways)])  63.1 us
    ppermute x16, waiting for transfers between devices, ring_gather(): lax.ppermute(going_up, axis, [(d, (d + 1) % ways) for d in range(ways)])  58.9 us
    dot_general x16, matrix products, cross(): lax.dot_general(left, right, (((1,), (1,)), ((), ())), preferred_element_...  23.3 us
    another operation x6, other arithmetic, block_step(): return (jnp.concatenate(pieces, axis=1), jnp.stack(grads))  7.92 us
  transfers between devices with their start and end apart: 32, of which 17 were waited for; matrix products, arithmetic and copies ran while one was open for 11% of the time, Pallas kernels for 0%

profile of v1, /device:TPU:0, one launch (start us, length us, event | category | flops | bytes accessed | tf_op | source)
XLA Modules:
  0.0 332.2 jit_solution(9403013032408039528)
XLA Ops:
  9.4 5.0 %collective-permute-start.1 = (bf16[2,3,32,512]{3,2,1,0:T(8,128)(2,1)}, bf16[2,3,32,512]{3,2,1,0:T(8,128)(2,1)S(1)}, u32[]{:S(2)}, u32[]{:S(2)}) collective-permute-start(bf16[2,3,32,512]{3,2,1,0:T(8,128)(2,1)} %get-tuple-element.9), channel_id=1, source_target_pairs={{0,15},{1,0},{2,1},{3,2},{4,3},{5,4},{6,5},{7,6},{8,7},{9,8},{10,9... | collective-permute-start | bytes 589832 | tf_op jit(solution)/shard_map/ppermute | solution.py:18
  20.2 4.4 %collective-permute-start.3 = (bf16[2,3,32,512]{3,2,1,0:T(8,128)(2,1)S(1)}, bf16[2,3,32,512]{3,2,1,0:T(8,128)(2,1)S(1)}, u32[]{:S(2)}, u32[]{:S(2)}) collective-permute-start(bf16[2,3,32,512]{3,2,1,0:T(8,128)(2,1)S(1)} %collective-permute-done.1), channel_id=1, source_target_pairs={{0,15},{1,0},{2,1},{3,2},{4,3},{5,4},{6,5},{7,6},{8,7},{9,8},{10,9... | collective-permute-start | bytes 589832 | tf_op jit(solution)/shard_map/ppermute | solution.py:18
  24.7 3.3 collective-permute-done.2
  28.0 4.5 %collective-permute-start.5 = (bf16[2,3,32,512]{3,2,1,0:T(8,128)(2,1)S(1)}, bf16[2,3,32,512]{3,2,1,0:T(8,128)(2,1)S(1)}, u32[]{:S(2)}, u32[]{:S(2)}) collective-permute-start(bf16[2,3,32,512]{3,2,1,0:T(8,128)(2,1)S(1)} %collective-permute-done.3), channel_id=1, source_target_pairs={{0,15},{1,0},{2,1},{3,2},{4,3},{5,4},{6,5},{7,6},{8,7},{9,8},{10,9... | collective-permute-start | bytes 589832 | tf_op jit(solution)/shard_map/ppermute | solution.py:18
  32.6 3.3 collective-permute-done.4
  35.9 4.5 %collective-permute-start.7 = (bf16[2,3,32,512]{3,2,1,0:T(8,128)(2,1)S(1)}, bf16[2,3,32,512]{3,2,1,0:T(8,128)(2,1)S(1)}, u32[]{:S(2)}, u32[]{:S(2)}) collective-permute-start(bf16[2,3,32,512]{3,2,1,0:T(8,128)(2,1)S(1)} %collective-permute-done.5), channel_id=1, source_target_pairs={{0,15},{1,0},{2,1},{3,2},{4,3},{5,4},{6,5},{7,6},{8,7},{9,8},{10,9... | collective-permute-start | bytes 589832 | tf_op jit(solution)/shard_map/ppermute | solution.py:18
  40.5 3.3 collective-permute-done.6
  43.8 4.5 %collective-permute-start.9 = (bf16[2,3,32,512]{3,2,1,0:T(8,128)(2,1)S(1)}, bf16[2,3,32,512]{3,2,1,0:T(8,128)(2,1)S(1)}, u32[]{:S(2)}, u32[]{:S(2)}) collective-permute-start(bf16[2,3,32,512]{3,2,1,0:T(8,128)(2,1)S(1)} %collective-permute-done.7), channel_id=1, source_target_pairs={{0,15},{1,0},{2,1},{3,2},{4,3},{5,4},{6,5},{7,6},{8,7},{9,8},{10,9... | collective-permute-start | bytes 589832 | tf_op jit(solution)/shard_map/ppermute | solution.py:18
  48.4 3.3 collective-permute-done.8
  51.7 4.4 %collective-permute-start.11 = (bf16[2,3,32,512]{3,2,1,0:T(8,128)(2,1)S(1)}, bf16[2,3,32,512]{3,2,1,0:T(8,128)(2,1)S(1)}, u32[]{:S(2)}, u32[]{:S(2)}) collective-permute-start(bf16[2,3,32,512]{3,2,1,0:T(8,128)(2,1)S(1)} %collective-permute-done.9), channel_id=1, source_target_pairs={{0,15},{1,0},{2,1},{3,2},{4,3},{5,4},{6,5},{7,6},{8,7},{9,8},{10,9... | collective-permute-start | bytes 589832 | tf_op jit(solution)/shard_map/ppermute | solution.py:18
  56.2 3.4 %collective-permute-done.10 = bf16[2,3,32,512]{3,2,1,0:T(8,128)(2,1)S(1)} collective-permute-done((bf16[2,3,32,512]{3,2,1,0:T(8,128)(2,1)S(1)}, bf16[2,3,32,512]{3,2,1,0:T(8,128)(2,1)S(1)}, u32[]{:S(2)}, u32[]{:S(2)}) %collective-permute-start.10) | collective-permute-done | bytes 196640 | tf_op jit(solution)/shard_map/ppermute | solution.py:15
  59.6 4.4 %collective-permute-start.13 = (bf16[2,3,32,512]{3,2,1,0:T(8,128)(2,1)S(1)}, bf16[2,3,32,512]{3,2,1,0:T(8,128)(2,1)S(1)}, u32[]{:S(2)}, u32[]{:S(2)}) collective-permute-start(bf16[2,3,32,512]{3,2,1,0:T(8,128)(2,1)S(1)} %collective-permute-done.11), channel_id=1, source_target_pairs={{0,15},{1,0},{2,1},{3,2},{4,3},{5,4},{6,5},{7,6},{8,7},{9,8},{10,9... | collective-permute-start | bytes 589832 | tf_op jit(solution)/shard_map/ppermute | solution.py:18
  64.1 3.3 collective-permute-done.12
  67.4 7.7 %collective-permute-done.14 = bf16[2,3,32,512]{3,2,1,0:T(8,128)(2,1)S(1)} collective-permute-done((bf16[2,3,32,512]{3,2,1,0:T(8,128)(2,1)S(1)}, bf16[2,3,32,512]{3,2,1,0:T(8,128)(2,1)S(1)}, u32[]{:S(2)}, u32[]{:S(2)}) %collective-permute-start.14) | collective-permute-done | bytes 196640 | tf_op jit(solution)/shard_map/ppermute | solution.py:15
  80.3 3.3 %pad_maximum_fusion = f32[2,3,512,512]{3,2,1,0:T(8,128)} fusion(f32[1,3,512,512]{3,2,1,0:T(8,128)S(1)} %maximum_bitcast_fusion.1, f32[1,3,512,512]{3,2,1,0:T(8,128)S(1)} %maximum_bitcast_fusion), kind=kLoop, calls=%fused_computation | loop fusion | flops 1572864 | bytes 12582912 | tf_op jit(solution)/shard_map/stack | solution.py:79
  83.8 82.9 %reduce-scatter.3.cloned.1.call-done = f32[2,3,32,512]{3,2,1,0:T(8,128)} async-done(((f32[2,3,512,512]{3,2,1,0:T(8,128)}), f32[2,3,32,512]{3,2,1,0:T(8,128)}) %reduce-scatter.3.cloned.1.call-update) | async-done | bytes 393232 | tf_op jit(solution)/shard_map/reduce_scatter | solution.py:87
  168.3 4.4 %collective-permute-start.16 = (bf16[2,3,32,512]{3,2,1,0:T(8,128)(2,1)S(1)}, bf16[2,3,32,512]{3,2,1,0:T(8,128)(2,1)S(1)}, u32[]{:S(2)}, u32[]{:S(2)}) collective-permute-start(bf16[2,3,32,512]{3,2,1,0:T(8,128)(2,1)S(1)} %get-tuple-element.5), channel_id=1, source_target_pairs={{0,15},{1,0},{2,1},{3,2},{4,3},{5,4},{6,5},{7,6},{8,7},{9,8},{10,9... | collective-permute-start | bytes 589832 | tf_op jit(solution)/shard_map/ppermute | solution.py:18
  172.7 3.5 %collective-permute-done.15 = bf16[2,3,32,512]{3,2,1,0:T(8,128)(2,1)S(1)} collective-permute-done((bf16[2,3,32,512]{3,2,1,0:T(8,128)(2,1)S(1)}, bf16[2,3,32,512]{3,2,1,0:T(8,128)(2,1)S(1)}, u32[]{:S(2)}, u32[]{:S(2)}) %collective-permute-start.15) | collective-permute-done | bytes 196640 | tf_op jit(solution)/shard_map/ppermute | solution.py:15
  176.2 4.4 %collective-permute-start.18 = (bf16[2,3,32,512]{3,2,1,0:T(8,128)(2,1)S(1)}, bf16[2,3,32,512]{3,2,1,0:T(8,128)(2,1)S(1)}, u32[]{:S(2)}, u32[]{:S(2)}) collective-permute-start(bf16[2,3,32,512]{3,2,1,0:T(8,128)(2,1)S(1)} %collective-permute-done.16), channel_id=1, source_target_pairs={{0,15},{1,0},{2,1},{3,2},{4,3},{5,4},{6,5},{7,6},{8,7},{9,8},{10,9... | collective-permute-start | bytes 589832 | tf_op jit(solution)/shard_map/ppermute | solution.py:18
  180.7 3.4 %collective-permute-done.17 = bf16[2,3,32,512]{3,2,1,0:T(8,128)(2,1)S(1)} collective-permute-done((bf16[2,3,32,512]{3,2,1,0:T(8,128)(2,1)S(1)}, bf16[2,3,32,512]{3,2,1,0:T(8,128)(2,1)S(1)}, u32[]{:S(2)}, u32[]{:S(2)}) %collective-permute-start.17) | collective-permute-done | bytes 196640 | tf_op jit(solution)/shard_map/ppermute | solution.py:15
  184.1 4.4 %collective-permute-start.20 = (bf16[2,3,32,512]{3,2,1,0:T(8,128)(2,1)S(1)}, bf16[2,3,32,512]{3,2,1,0:T(8,128)(2,1)S(1)}, u32[]{:S(2)}, u32[]{:S(2)}) collective-permute-start(bf16[2,3,32,512]{3,2,1,0:T(8,128)(2,1)S(1)} %collective-permute-done.18), channel_id=1, source_target_pairs={{0,15},{1,0},{2,1},{3,2},{4,3},{5,4},{6,5},{7,6},{8,7},{9,8},{10,9... | collective-permute-start | bytes 589832 | tf_op jit(solution)/shard_map/ppermute | solution.py:18
  188.6 3.3 collective-permute-done.19
  191.9 4.5 %collective-permute-start.22 = (bf16[2,3,32,512]{3,2,1,0:T(8,128)(2,1)S(1)}, bf16[2,3,32,512]{3,2,1,0:T(8,128)(2,1)S(1)}, u32[]{:S(2)}, u32[]{:S(2)}) collective-permute-start(bf16[2,3,32,512]{3,2,1,0:T(8,128)(2,1)S(1)} %collective-permute-done.20), channel_id=1, source_target_pairs={{0,15},{1,0},{2,1},{3,2},{4,3},{5,4},{6,5},{7,6},{8,7},{9,8},{10,9... | collective-permute-start | bytes 589832 | tf_op jit(solution)/shard_map/ppermute | solution.py:18
  196.4 3.3 collective-permute-done.21
  199.7 4.4 %collective-permute-start.24 = (bf16[2,3,32,512]{3,2,1,0:T(8,128)(2,1)S(1)}, bf16[2,3,32,512]{3,2,1,0:T(8,128)(2,1)S(1)}, u32[]{:S(2)}, u32[]{:S(2)}) collective-permute-start(bf16[2,3,32,512]{3,2,1,0:T(8,128)(2,1)S(1)} %collective-permute-done.22), channel_id=1, source_target_pairs={{0,15},{1,0},{2,1},{3,2},{4,3},{5,4},{6,5},{7,6},{8,7},{9,8},{10,9... | collective-permute-start | bytes 589832 | tf_op jit(solution)/shard_map/ppermute | solution.py:18
  204.2 3.4 %collective-permute-done.23 = bf16[2,3,32,512]{3,2,1,0:T(8,128)(2,1)S(1)} collective-permute-done((bf16[2,3,32,512]{3,2,1,0:T(8,128)(2,1)S(1)}, bf16[2,3,32,512]{3,2,1,0:T(8,128)(2,1)S(1)}, u32[]{:S(2)}, u32[]{:S(2)}) %collective-permute-start.23) | collective-permute-done | bytes 196640 | tf_op jit(solution)/shard_map/ppermute | solution.py:15
  207.6 4.4 %collective-permute-start.26 = (bf16[2,3,32,512]{3,2,1,0:T(8,128)(2,1)S(1)}, bf16[2,3,32,512]{3,2,1,0:T(8,128)(2,1)S(1)}, u32[]{:S(2)}, u32[]{:S(2)}) collective-permute-start(bf16[2,3,32,512]{3,2,1,0:T(8,128)(2,1)S(1)} %collective-permute-done.24), channel_id=1, source_target_pairs={{0,15},{1,0},{2,1},{3,2},{4,3},{5,4},{6,5},{7,6},{8,7},{9,8},{10,9... | collective-permute-start | bytes 589832 | tf_op jit(solution)/shard_map/ppermute | solution.py:18
  212.1 3.4 %collective-permute-done.25 = bf16[2,3,32,512]{3,2,1,0:T(8,128)(2,1)S(1)} collective-permute-done((bf16[2,3,32,512]{3,2,1,0:T(8,128)(2,1)S(1)}, bf16[2,3,32,512]{3,2,1,0:T(8,128)(2,1)S(1)}, u32[]{:S(2)}, u32[]{:S(2)}) %collective-permute-start.25) | collective-permute-done | bytes 196640 | tf_op jit(solution)/shard_map/ppermute | solution.py:15
  215.5 4.4 %collective-permute-start.28 = (bf16[2,3,32,512]{3,2,1,0:T(8,128)(2,1)S(1)}, bf16[2,3,32,512]{3,2,1,0:T(8,128)(2,1)S(1)}, u32[]{:S(2)}, u32[]{:S(2)}) collective-permute-start(bf16[2,3,32,512]{3,2,1,0:T(8,128)(2,1)S(1)} %collective-permute-done.26), channel_id=1, source_target_pairs={{0,15},{1,0},{2,1},{3,2},{4,3},{5,4},{6,5},{7,6},{8,7},{9,8},{10,9... | collective-permute-start | bytes 589832 | tf_op jit(solution)/shard_map/ppermute | solution.py:18
  223.4 7.7 %collective-permute-done.29 = bf16[2,3,32,512]{3,2,1,0:T(8,128)(2,1)S(1)} collective-permute-done((bf16[2,3,32,512]{3,2,1,0:T(8,128)(2,1)S(1)}, bf16[2,3,32,512]{3,2,1,0:T(8,128)(2,1)S(1)}, u32[]{:S(2)}, u32[]{:S(2)}) %collective-permute-start.29) | collective-permute-done | bytes 196640 | tf_op jit(solution)/shard_map/ppermute | solution.py:15
  236.4 3.3 %pad_maximum_fusion.1 = f32[2,3,512,512]{3,2,1,0:T(8,128)} fusion(f32[1,3,512,512]{3,2,1,0:T(8,128)S(1)} %maximum_bitcast_fusion.3, f32[1,3,512,512]{3,2,1,0:T(8,128)S(1)} %maximum_bitcast_fusion.2), kind=kLoop, calls=%fused_computation.1 | loop fusion | flops 1572864 | bytes 12582912 | tf_op jit(solution)/shard_map/stack | solution.py:79
  269.6 52.6 %reduce-scatter.5.cloned.1.call-done = f32[2,3,32,512]{3,2,1,0:T(8,128)} async-done(((f32[2,3,512,512]{3,2,1,0:T(8,128)}), f32[2,3,32,512]{3,2,1,0:T(8,128)}) %reduce-scatter.5.cloned.1.call-update) | async-done | bytes 393232 | tf_op jit(solution)/shard_map/reduce_scatter | solution.py:87
  (152 shorter events, 56.6 us)
Async XLA Ops:
  7.2 159.5 %reduce-scatter.3.cloned.1.call-start = ((), (), s32[]{:S(2)}) async-start(), calls=%async_computation.2 | async-start | bytes 6684672 | tf_op jit(solution)/shard_map/reduce_scatter | solution.py:87
  8.9 11.3 %collective-permute-start = (bf16[2,3,32,512]{3,2,1,0:T(8,128)(2,1)}, bf16[2,3,32,512]{3,2,1,0:T(8,128)(2,1)S(1)}, u32[]{:S(2)}, u32[]{:S(2)}) collective-permute-start(bf16[2,3,32,512]{3,2,1,0:T(8,128)(2,1)} %get-tuple-element.9), channel_id=1, source_target_pairs={{0,1},{1,2},{2,3},{3,4},{4,5},{5,6},{6,7},{7,8},{8,9},{9,10},{10,1... | collective-permute-start | bytes 589832 | tf_op jit(solution)/shard_map/ppermute | solution.py:15
  9.4 10.8 %collective-permute-start.1 = (bf16[2,3,32,512]{3,2,1,0:T(8,128)(2,1)}, bf16[2,3,32,512]{3,2,1,0:T(8,128)(2,1)S(1)}, u32[]{:S(2)}, u32[]{:S(2)}) collective-permute-start(bf16[2,3,32,512]{3,2,1,0:T(8,128)(2,1)} %get-tuple-element.9), channel_id=1, source_target_pairs={{0,15},{1,0},{2,1},{3,2},{4,3},{5,4},{6,5},{7,6},{8,7},{9,8},{10,9... | collective-permute-start | bytes 589832 | tf_op jit(solution)/shard_map/ppermute | solution.py:18
  20.1 7.9 %collective-permute-start.2 = (bf16[2,3,32,512]{3,2,1,0:T(8,128)(2,1)S(1)}, bf16[2,3,32,512]{3,2,1,0:T(8,128)(2,1)S(1)}, u32[]{:S(2)}, u32[]{:S(2)}) collective-permute-start(bf16[2,3,32,512]{3,2,1,0:T(8,128)(2,1)S(1)} %collective-permute-done), channel_id=1, source_target_pairs={{0,1},{1,2},{2,3},{3,4},{4,5},{5,6},{6,7},{7,8},{8,9},{9,10},{10,1... | collective-permute-start | bytes 589832 | tf_op jit(solution)/shard_map/ppermute | solution.py:15
  20.2 7.8 %collective-permute-start.3 = (bf16[2,3,32,512]{3,2,1,0:T(8,128)(2,1)S(1)}, bf16[2,3,32,512]{3,2,1,0:T(8,128)(2,1)S(1)}, u32[]{:S(2)}, u32[]{:S(2)}) collective-permute-start(bf16[2,3,32,512]{3,2,1,0:T(8,128)(2,1)S(1)} %collective-permute-done.1), channel_id=1, source_target_pairs={{0,15},{1,0},{2,1},{3,2},{4,3},{5,4},{6,5},{7,6},{8,7},{9,8},{10,9... | collective-permute-start | bytes 589832 | tf_op jit(solution)/shard_map/ppermute | solution.py:18
  28.0 7.9 %collective-permute-start.4 = (bf16[2,3,32,512]{3,2,1,0:T(8,128)(2,1)S(1)}, bf16[2,3,32,512]{3,2,1,0:T(8,128)(2,1)S(1)}, u32[]{:S(2)}, u32[]{:S(2)}) collective-permute-start(bf16[2,3,32,512]{3,2,1,0:T(8,128)(2,1)S(1)} %collective-permute-done.2), channel_id=1, source_target_pairs={{0,1},{1,2},{2,3},{3,4},{4,5},{5,6},{6,7},{7,8},{8,9},{9,10},{10,1... | collective-permute-start | bytes 589832 | tf_op jit(solution)/shard_map/ppermute | solution.py:15
  28.0 7.9 %collective-permute-start.5 = (bf16[2,3,32,512]{3,2,1,0:T(8,128)(2,1)S(1)}, bf16[2,3,32,512]{3,2,1,0:T(8,128)(2,1)S(1)}, u32[]{:S(2)}, u32[]{:S(2)}) collective-permute-start(bf16[2,3,32,512]{3,2,1,0:T(8,128)(2,1)S(1)} %collective-permute-done.3), channel_id=1, source_target_pairs={{0,15},{1,0},{2,1},{3,2},{4,3},{5,4},{6,5},{7,6},{8,7},{9,8},{10,9... | collective-permute-start | bytes 589832 | tf_op jit(solution)/shard_map/ppermute | solution.py:18
  35.9 7.9 %collective-permute-start.6 = (bf16[2,3,32,512]{3,2,1,0:T(8,128)(2,1)S(1)}, bf16[2,3,32,512]{3,2,1,0:T(8,128)(2,1)S(1)}, u32[]{:S(2)}, u32[]{:S(2)}) collective-permute-start(bf16[2,3,32,512]{3,2,1,0:T(8,128)(2,1)S(1)} %collective-permute-done.4), channel_id=1, source_target_pairs={{0,1},{1,2},{2,3},{3,4},{4,5},{5,6},{6,7},{7,8},{8,9},{9,10},{10,1... | collective-permute-start | bytes 589832 | tf_op jit(solution)/shard_map/ppermute | solution.py:15
  35.9 7.9 %collective-permute-start.7 = (bf16[2,3,32,512]{3,2,1,0:T(8,128)(2,1)S(1)}, bf16[2,3,32,512]{3,2,1,0:T(8,128)(2,1)S(1)}, u32[]{:S(2)}, u32[]{:S(2)}) collective-permute-start(bf16[2,3,32,512]{3,2,1,0:T(8,128)(2,1)S(1)} %collective-permute-done.5), channel_id=1, source_target_pairs={{0,15},{1,0},{2,1},{3,2},{4,3},{5,4},{6,5},{7,6},{8,7},{9,8},{10,9... | collective-permute-start | bytes 589832 | tf_op jit(solution)/shard_map/ppermute | solution.py:18
  43.8 7.9 %collective-permute-start.8 = (bf16[2,3,32,512]{3,2,1,0:T(8,128)(2,1)S(1)}, bf16[2,3,32,512]{3,2,1,0:T(8,128)(2,1)S(1)}, u32[]{:S(2)}, u32[]{:S(2)}) collective-permute-start(bf16[2,3,32,512]{3,2,1,0:T(8,128)(2,1)S(1)} %collective-permute-done.6), channel_id=1, source_target_pairs={{0,1},{1,2},{2,3},{3,4},{4,5},{5,6},{6,7},{7,8},{8,9},{9,10},{10,1... | collective-permute-start | bytes 589832 | tf_op jit(solution)/shard_map/ppermute | solution.py:15
  43.8 7.9 %collective-permute-start.9 = (bf16[2,3,32,512]{3,2,1,0:T(8,128)(2,1)S(1)}, bf16[2,3,32,512]{3,2,1,0:T(8,128)(2,1)S(1)}, u32[]{:S(2)}, u32[]{:S(2)}) collective-permute-start(bf16[2,3,32,512]{3,2,1,0:T(8,128)(2,1)S(1)} %collective-permute-done.7), channel_id=1, source_target_pairs={{0,15},{1,0},{2,1},{3,2},{4,3},{5,4},{6,5},{7,6},{8,7},{9,8},{10,9... | collective-permute-start | bytes 589832 | tf_op jit(solution)/shard_map/ppermute | solution.py:18
  51.7 7.9 %collective-permute-start.10 = (bf16[2,3,32,512]{3,2,1,0:T(8,128)(2,1)S(1)}, bf16[2,3,32,512]{3,2,1,0:T(8,128)(2,1)S(1)}, u32[]{:S(2)}, u32[]{:S(2)}) collective-permute-start(bf16[2,3,32,512]{3,2,1,0:T(8,128)(2,1)S(1)} %collective-permute-done.8), channel_id=1, source_target_pairs={{0,1},{1,2},{2,3},{3,4},{4,5},{5,6},{6,7},{7,8},{8,9},{9,10},{10,1... | collective-permute-start | bytes 589832 | tf_op jit(solution)/shard_map/ppermute | solution.py:15
  51.7 7.9 %collective-permute-start.11 = (bf16[2,3,32,512]{3,2,1,0:T(8,128)(2,1)S(1)}, bf16[2,3,32,512]{3,2,1,0:T(8,128)(2,1)S(1)}, u32[]{:S(2)}, u32[]{:S(2)}) collective-permute-start(bf16[2,3,32,512]{3,2,1,0:T(8,128)(2,1)S(1)} %collective-permute-done.9), channel_id=1, source_target_pairs={{0,15},{1,0},{2,1},{3,2},{4,3},{5,4},{6,5},{7,6},{8,7},{9,8},{10,9... | collective-permute-start | bytes 589832 | tf_op jit(solution)/shard_map/ppermute | solution.py:18
  59.6 7.8 %collective-permute-start.12 = (bf16[2,3,32,512]{3,2,1,0:T(8,128)(2,1)S(1)}, bf16[2,3,32,512]{3,2,1,0:T(8,128)(2,1)S(1)}, u32[]{:S(2)}, u32[]{:S(2)}) collective-permute-start(bf16[2,3,32,512]{3,2,1,0:T(8,128)(2,1)S(1)} %collective-permute-done.10), channel_id=1, source_target_pairs={{0,1},{1,2},{2,3},{3,4},{4,5},{5,6},{6,7},{7,8},{8,9},{9,10},{10,1... | collective-permute-start | bytes 589832 | tf_op jit(solution)/shard_map/ppermute | solution.py:15
  59.6 7.8 %collective-permute-start.13 = (bf16[2,3,32,512]{3,2,1,0:T(8,128)(2,1)S(1)}, bf16[2,3,32,512]{3,2,1,0:T(8,128)(2,1)S(1)}, u32[]{:S(2)}, u32[]{:S(2)}) collective-permute-start(bf16[2,3,32,512]{3,2,1,0:T(8,128)(2,1)S(1)} %collective-permute-done.11), channel_id=1, source_target_pairs={{0,15},{1,0},{2,1},{3,2},{4,3},{5,4},{6,5},{7,6},{8,7},{9,8},{10,9... | collective-permute-start | bytes 589832 | tf_op jit(solution)/shard_map/ppermute | solution.py:18
  67.4 7.8 %collective-permute-start.14 = (bf16[2,3,32,512]{3,2,1,0:T(8,128)(2,1)S(1)}, bf16[2,3,32,512]{3,2,1,0:T(8,128)(2,1)S(1)}, u32[]{:S(2)}, u32[]{:S(2)}) collective-permute-start(bf16[2,3,32,512]{3,2,1,0:T(8,128)(2,1)S(1)} %collective-permute-done.12), channel_id=1, source_target_pairs={{0,1},{1,2},{2,3},{3,4},{4,5},{5,6},{6,7},{7,8},{8,9},{9,10},{10,1... | collective-permute-start | bytes 589832 | tf_op jit(solution)/shard_map/ppermute | solution.py:15
  83.7 238.5 %reduce-scatter.5.cloned.1.call-start = ((), (), s32[]{:S(2)}) async-start(), calls=%async_computation.3 | async-start | bytes 6684672 | tf_op jit(solution)/shard_map/reduce_scatter | solution.py:87
  168.2 7.9 %collective-permute-start.15 = (bf16[2,3,32,512]{3,2,1,0:T(8,128)(2,1)S(1)}, bf16[2,3,32,512]{3,2,1,0:T(8,128)(2,1)S(1)}, u32[]{:S(2)}, u32[]{:S(2)}) collective-permute-start(bf16[2,3,32,512]{3,2,1,0:T(8,128)(2,1)S(1)} %get-tuple-element.5), channel_id=1, source_target_pairs={{0,1},{1,2},{2,3},{3,4},{4,5},{5,6},{6,7},{7,8},{8,9},{9,10},{10,1... | collective-permute-start | bytes 589832 | tf_op jit(solution)/shard_map/ppermute | solution.py:15
  168.3 7.9 %collective-permute-start.16 = (bf16[2,3,32,512]{3,2,1,0:T(8,128)(2,1)S(1)}, bf16[2,3,32,512]{3,2,1,0:T(8,128)(2,1)S(1)}, u32[]{:S(2)}, u32[]{:S(2)}) collective-permute-start(bf16[2,3,32,512]{3,2,1,0:T(8,128)(2,1)S(1)} %get-tuple-element.5), channel_id=1, source_target_pairs={{0,15},{1,0},{2,1},{3,2},{4,3},{5,4},{6,5},{7,6},{8,7},{9,8},{10,9... | collective-permute-start | bytes 589832 | tf_op jit(solution)/shard_map/ppermute | solution.py:18
  176.2 7.9 %collective-permute-start.17 = (bf16[2,3,32,512]{3,2,1,0:T(8,128)(2,1)S(1)}, bf16[2,3,32,512]{3,2,1,0:T(8,128)(2,1)S(1)}, u32[]{:S(2)}, u32[]{:S(2)}) collective-permute-start(bf16[2,3,32,512]{3,2,1,0:T(8,128)(2,1)S(1)} %collective-permute-done.15), channel_id=1, source_target_pairs={{0,1},{1,2},{2,3},{3,4},{4,5},{5,6},{6,7},{7,8},{8,9},{9,10},{10,1... | collective-permute-start | bytes 589832 | tf_op jit(solution)/shard_map/ppermute | solution.py:15
  176.2 7.9 %collective-permute-start.18 = (bf16[2,3,32,512]{3,2,1,0:T(8,128)(2,1)S(1)}, bf16[2,3,32,512]{3,2,1,0:T(8,128)(2,1)S(1)}, u32[]{:S(2)}, u32[]{:S(2)}) collective-permute-start(bf16[2,3,32,512]{3,2,1,0:T(8,128)(2,1)S(1)} %collective-permute-done.16), channel_id=1, source_target_pairs={{0,15},{1,0},{2,1},{3,2},{4,3},{5,4},{6,5},{7,6},{8,7},{9,8},{10,9... | collective-permute-start | bytes 589832 | tf_op jit(solution)/shard_map/ppermute | solution.py:18
  184.1 7.8 %collective-permute-start.19 = (bf16[2,3,32,512]{3,2,1,0:T(8,128)(2,1)S(1)}, bf16[2,3,32,512]{3,2,1,0:T(8,128)(2,1)S(1)}, u32[]{:S(2)}, u32[]{:S(2)}) collective-permute-start(bf16[2,3,32,512]{3,2,1,0:T(8,128)(2,1)S(1)} %collective-permute-done.17), channel_id=1, source_target_pairs={{0,1},{1,2},{2,3},{3,4},{4,5},{5,6},{6,7},{7,8},{8,9},{9,10},{10,1... | collective-permute-start | bytes 589832 | tf_op jit(solution)/shard_map/ppermute | solution.py:15
  184.1 7.8 %collective-permute-start.20 = (bf16[2,3,32,512]{3,2,1,0:T(8,128)(2,1)S(1)}, bf16[2,3,32,512]{3,2,1,0:T(8,128)(2,1)S(1)}, u32[]{:S(2)}, u32[]{:S(2)}) collective-permute-start(bf16[2,3,32,512]{3,2,1,0:T(8,128)(2,1)S(1)} %collective-permute-done.18), channel_id=1, source_target_pairs={{0,15},{1,0},{2,1},{3,2},{4,3},{5,4},{6,5},{7,6},{8,7},{9,8},{10,9... | collective-permute-start | bytes 589832 | tf_op jit(solution)/shard_map/ppermute | solution.py:18
  191.8 7.9 %collective-permute-start.21 = (bf16[2,3,32,512]{3,2,1,0:T(8,128)(2,1)S(1)}, bf16[2,3,32,512]{3,2,1,0:T(8,128)(2,1)S(1)}, u32[]{:S(2)}, u32[]{:S(2)}) collective-permute-start(bf16[2,3,32,512]{3,2,1,0:T(8,128)(2,1)S(1)} %collective-permute-done.19), channel_id=1, source_target_pairs={{0,1},{1,2},{2,3},{3,4},{4,5},{5,6},{6,7},{7,8},{8,9},{9,10},{10,1... | collective-permute-start | bytes 589832 | tf_op jit(solution)/shard_map/ppermute | solution.py:15
  191.9 7.9 %collective-permute-start.22 = (bf16[2,3,32,512]{3,2,1,0:T(8,128)(2,1)S(1)}, bf16[2,3,32,512]{3,2,1,0:T(8,128)(2,1)S(1)}, u32[]{:S(2)}, u32[]{:S(2)}) collective-permute-start(bf16[2,3,32,512]{3,2,1,0:T(8,128)(2,1)S(1)} %collective-permute-done.20), channel_id=1, source_target_pairs={{0,15},{1,0},{2,1},{3,2},{4,3},{5,4},{6,5},{7,6},{8,7},{9,8},{10,9... | collective-permute-start | bytes 589832 | tf_op jit(solution)/shard_map/ppermute | solution.py:18
  199.7 7.9 %collective-permute-start.23 = (bf16[2,3,32,512]{3,2,1,0:T(8,128)(2,1)S(1)}, bf16[2,3,32,512]{3,2,1,0:T(8,128)(2,1)S(1)}, u32[]{:S(2)}, u32[]{:S(2)}) collective-permute-start(bf16[2,3,32,512]{3,2,1,0:T(8,128)(2,1)S(1)} %collective-permute-done.21), channel_id=1, source_target_pairs={{0,1},{1,2},{2,3},{3,4},{4,5},{5,6},{6,7},{7,8},{8,9},{9,10},{10,1... | collective-permute-start | bytes 589832 | tf_op jit(solution)/shard_map/ppermute | solution.py:15
  199.7 7.9 %collective-permute-start.24 = (bf16[2,3,32,512]{3,2,1,0:T(8,128)(2,1)S(1)}, bf16[2,3,32,512]{3,2,1,0:T(8,128)(2,1)S(1)}, u32[]{:S(2)}, u32[]{:S(2)}) collective-permute-start(bf16[2,3,32,512]{3,2,1,0:T(8,128)(2,1)S(1)} %collective-permute-done.22), channel_id=1, source_target_pairs={{0,15},{1,0},{2,1},{3,2},{4,3},{5,4},{6,5},{7,6},{8,7},{9,8},{10,9... | collective-permute-start | bytes 589832 | tf_op jit(solution)/shard_map/ppermute | solution.py:18
  207.6 7.9 %collective-permute-start.25 = (bf16[2,3,32,512]{3,2,1,0:T(8,128)(2,1)S(1)}, bf16[2,3,32,512]{3,2,1,0:T(8,128)(2,1)S(1)}, u32[]{:S(2)}, u32[]{:S(2)}) collective-permute-start(bf16[2,3,32,512]{3,2,1,0:T(8,128)(2,1)S(1)} %collective-permute-done.23), channel_id=1, source_target_pairs={{0,1},{1,2},{2,3},{3,4},{4,5},{5,6},{6,7},{7,8},{8,9},{9,10},{10,1... | collective-permute-start | bytes 589832 | tf_op jit(solution)/shard_map/ppermute | solution.py:15
  207.6 7.9 %collective-permute-start.26 = (bf16[2,3,32,512]{3,2,1,0:T(8,128)(2,1)S(1)}, bf16[2,3,32,512]{3,2,1,0:T(8,128)(2,1)S(1)}, u32[]{:S(2)}, u32[]{:S(2)}) collective-permute-start(bf16[2,3,32,512]{3,2,1,0:T(8,128)(2,1)S(1)} %collective-permute-done.24), channel_id=1, source_target_pairs={{0,15},{1,0},{2,1},{3,2},{4,3},{5,4},{6,5},{7,6},{8,7},{9,8},{10,9... | collective-permute-start | bytes 589832 | tf_op jit(solution)/shard_map/ppermute | solution.py:18
  215.5 7.8 %collective-permute-start.27 = (bf16[2,3,32,512]{3,2,1,0:T(8,128)(2,1)S(1)}, bf16[2,3,32,512]{3,2,1,0:T(8,128)(2,1)S(1)}, u32[]{:S(2)}, u32[]{:S(2)}) collective-permute-start(bf16[2,3,32,512]{3,2,1,0:T(8,128)(2,1)S(1)} %collective-permute-done.25), channel_id=1, source_target_pairs={{0,1},{1,2},{2,3},{3,4},{4,5},{5,6},{6,7},{7,8},{8,9},{9,10},{10,1... | collective-permute-start | bytes 589832 | tf_op jit(solution)/shard_map/ppermute | solution.py:15
  215.5 7.8 %collective-permute-start.28 = (bf16[2,3,32,512]{3,2,1,0:T(8,128)(2,1)S(1)}, bf16[2,3,32,512]{3,2,1,0:T(8,128)(2,1)S(1)}, u32[]{:S(2)}, u32[]{:S(2)}) collective-permute-start(bf16[2,3,32,512]{3,2,1,0:T(8,128)(2,1)S(1)} %collective-permute-done.26), channel_id=1, source_target_pairs={{0,15},{1,0},{2,1},{3,2},{4,3},{5,4},{6,5},{7,6},{8,7},{9,8},{10,9... | collective-permute-start | bytes 589832 | tf_op jit(solution)/shard_map/ppermute | solution.py:18
  223.3 7.8 %collective-permute-start.29 = (bf16[2,3,32,512]{3,2,1,0:T(8,128)(2,1)S(1)}, bf16[2,3,32,512]{3,2,1,0:T(8,128)(2,1)S(1)}, u32[]{:S(2)}, u32[]{:S(2)}) collective-permute-start(bf16[2,3,32,512]{3,2,1,0:T(8,128)(2,1)S(1)} %collective-permute-done.27), channel_id=1, source_target_pairs={{0,1},{1,2},{2,3},{3,4},{4,5},{5,6},{6,7},{7,8},{8,9},{9,10},{10,1... | collective-permute-start | bytes 589832 | tf_op jit(solution)/shard_map/ppermute | solution.py:15
  (13 other events, 235.6 us)
Sparse Core Ops, SparseCore 0:
  83.8 82.7 reduce-scatter.2
  239.9 82.3 reduce-scatter.4
